TPU v7x, 768 devices: a whole 4x8x12 slice. The times are simulated.
768 devices in a mesh: ctx: 32 (over y, z_hi), tp: 24 (over z_lo, x, core).
Axes of the slice: x: 4, y: 8, z: 12 (z_hi: 4, z_lo: 3; z = z_hi * 3 + z_lo), core: 2. Of those that a mesh axis runs over, the one named last changes fastest.
Arguments:
- tokens: bfloat16 [16384, 5376], P('ctx'), may hold values from -36 to 36, as said below
- norm_gain: float32 [5376], replicated, may hold values from 0.5 to 1.5
- query_weight: bfloat16 [5376, 3072], P(None, 'tp'), may hold values from -0.078125 to 0.078125
- keyval_weight: bfloat16 [5376, 3072], P(None, 'tp'), may hold values from -0.07637626 to 0.07637626
- query_gain: float32 [128], replicated, may hold values from 0.5 to 40
- key_gain: float32 [128], replicated, may hold values from 0.5 to 40
- out_weight: bfloat16 [3072, 5376], P('tp'), may hold values from -2.8 to 2.8
- post_gain: float32 [5376], P('tp'), may hold values from 0.5 to 1.5
Outputs:
- layer_out: bfloat16 [16384, 5376], P('ctx', 'tp')
Inputs may be any that keep to these rules, and one draw needn't show every extreme that they name: `tokens`: each row and feature has its own scale.
All inputs are finite; a program needn't handle non-finite values.
Results may differ from a plain program's by a relative error of at most 0.03.
Values may be sent and summed in bfloat16 or wider, within the bound.
No kernel may reach another device: no remote copies, remote signals or barrier semaphores. Data moves between devices by JAX's collectives and lax.ppermute only.
A program may use at most 128 MiB of HBM per device.

v0:
```python
import jax
import jax.numpy as jnp
from jax import lax
from jax.sharding import PartitionSpec as P

WIN = 1024


epsilon = 1e-06
query_scalar = 168.0
rope_base = 10000.0


def padded(cells, sides, width):
    for axis, dim in sides:
        count = lax.axis_size(axis)
        ends = count - 1
        head = lax.slice_in_dim(cells, 0, width, axis=dim)
        tail = lax.slice_in_dim(cells, cells.shape[dim] - width, cells.shape[dim], axis=dim)
        cells = jnp.concatenate(
            [
                lax.ppermute(tail, axis, [(i, (i + 1) % count) for i in range(ends)]),
                cells,
                lax.ppermute(head, axis, [((i + 1) % count, i) for i in range(ends)]),
            ],
            axis=dim,
        )
    return cells


def from_behind(block, axis, distance):
    devices = range(lax.axis_size(axis))
    route = [(i - distance, i) for i in devices if i - distance in devices]
    return lax.ppermute(block, axis, route)


def rope_tables(positions, head_width):
    half_width = head_width // 2
    exponent = jnp.arange(half_width, dtype=jnp.float32) * (2.0 / head_width)
    frequency = rope_base ** (-exponent)
    angles = positions.astype(jnp.float32)[:, None] * frequency[None, :]
    cosine = jnp.concatenate([jnp.cos(angles), jnp.cos(angles)], axis=1)
    sine_table = jnp.concatenate([jnp.sin(angles), jnp.sin(angles)], axis=1)
    return (cosine, sine_table)


def rotate(signal, cosine, sine_table):
    half_width = signal.shape[-1] // 2
    turned = jnp.concatenate([-signal[:, half_width:], signal[:, :half_width]], axis=1)
    return signal * cosine + turned * sine_table


def rms_scale(signal, gain_vector):
    return (
        signal
        * lax.rsqrt(jnp.mean(signal * signal, axis=-1, keepdims=True) + epsilon)
        * gain_vector
    )


def body(
    tokens, norm_gain, query_weight, keyval_weight, query_gain, key_gain, out_weight, post_gain
):
    tok_rows = tokens.shape[0]
    model_width = tokens.shape[1]
    head_width = query_weight.shape[1]
    col_share = post_gain.shape[0]
    ctx_index = lax.axis_index("ctx")
    tp_index = lax.axis_index("tp")
    as_float = tokens.astype(jnp.float32)
    normed = rms_scale(as_float, norm_gain).astype(jnp.bfloat16)
    positions = ctx_index * tok_rows + jnp.arange(tok_rows, dtype=jnp.int32)
    cosine, sine_table = rope_tables(positions, head_width)
    queries = jnp.dot(normed, query_weight, preferred_element_type=jnp.float32)
    queries = (
        rotate(rms_scale(queries, query_gain), cosine, sine_table) * query_scalar ** (-0.5)
    ).astype(jnp.bfloat16)
    projected = jnp.dot(normed, keyval_weight, preferred_element_type=jnp.float32)
    is_even = tp_index % 2 == 0
    rotated = rotate(rms_scale(projected, key_gain), cosine, sine_table)
    own_block = jnp.where(is_even, rotated, projected).astype(jnp.bfloat16)
    framed = padded(own_block, (("tp", 1),), head_width)
    lower_rim = framed[:, :head_width]
    upper_rim = framed[:, 2 * head_width :]
    key_rows = jnp.where(is_even, own_block, lower_rim)
    value_rows = jnp.where(is_even, upper_rim, own_block)
    paired = jnp.concatenate([key_rows, value_rows], axis=1)
    span_count = WIN // tok_rows
    earlier = []
    for offset in range(span_count, 0, -1):
        earlier.append(from_behind(paired, "ctx", offset))
    window = jnp.concatenate(earlier + [paired], axis=0)
    key_pos = ctx_index * tok_rows - WIN + jnp.arange(WIN + tok_rows, dtype=jnp.int32)
    distance = positions[:, None] - key_pos[None, :]
    allowed = (key_pos[None, :] >= 0) & (distance >= 0) & (distance < WIN)
    scores = lax.dot_general(
        queries,
        window[:, :head_width],
        (((1,), (1,)), ((), ())),
        preferred_element_type=jnp.float32,
    )
    scores = jnp.where(allowed, scores, -1e30)
    row_max = jnp.max(scores, axis=1, keepdims=True)
    lifted = jnp.exp(scores - row_max)
    weights = (lifted / jnp.sum(lifted, axis=1, keepdims=True)).astype(jnp.bfloat16)
    attended = jnp.dot(weights, window[:, head_width:], preferred_element_type=jnp.float32).astype(
        jnp.bfloat16
    )
    partial_sum = jnp.dot(attended, out_weight, preferred_element_type=jnp.float32)
    summed = lax.psum_scatter(
        partial_sum.astype(jnp.bfloat16), "tp", scatter_dimension=1, tiled=True
    ).astype(jnp.float32)
    squares = lax.psum(jnp.sum(summed * summed, axis=1), "tp")
    scaled = summed * lax.rsqrt(squares[:, None] / model_width + epsilon) * post_gain
    residual = lax.dynamic_slice_in_dim(as_float, tp_index * col_share, col_share, 1)
    return (residual + scaled).astype(jnp.bfloat16)


def solution(mesh):
    return jax.shard_map(
        body,
        mesh=mesh,
        in_specs=(
            P("ctx", None),
            P(),
            P(None, "tp"),
            P(None, "tp"),
            P(),
            P(),
            P("tp", None),
            P("tp"),
        ),
        out_specs=P("ctx", "tp"),
        check_vma=False,
    )
```

profile of v0, /device:TPU:208, one launch (start us, length us, event | category | flops | bytes accessed | tf_op | source)
XLA Modules:
  0.0 284.0 jit_solution(8413077586828066374)
XLA Ops:
  6.5 0.0 copy-start
  6.5 0.0 reduce-scatter.2.cloned.1.call-start
  6.6 8.4 %copy.9 = bf16[512,5376]{0,1:T(8,128)(2,1)} copy(bf16[512,5376]{1,0:T(8,128)(2,1)} %param.8) | data formatting | bytes 11010048 | tf_op args[0]
  15.0 3.8 %multiply_reduce_fusion = f32[512]{0:T(512)S(1)} fusion(bf16[512,5376]{0,1:T(8,128)(2,1)} %copy.9), kind=kLoop, calls=%fused_computation.1 | loop fusion | flops 8257024 | bytes 5507072 | tf_op jit(solution)/shard_map/reduce_sum | solution.py:56
  18.8 0.0 copy-start.2
  18.8 4.9 %multiply_reduce_fusion.1 = (f32[512]{0:T(512)S(1)}, f32[512,128]{0,1:T(8,128)S(1)}) fusion(bf16[5376,128]{1,0:T(8,128)(2,1)} %param.11, f32[5376]{0:T(1024)S(1)} %copy-done.5, f32[512]{0:T(512)S(1)} %add_rsqrt_fusion.3, bf16[512,5376]{0,1:T(8,128)(2,1)} %copy.9), kind=kOutput, calls=%fused_computation.38 | convolution fusion | flops 715783680 | bytes 7169024 | tf_op jit(solution)/shard_map/dot_general | solution.py:78
  23.8 0.1 multiply_multiply_fusion
  23.9 0.5 multiply_sine_fusion
  24.4 0.1 fusion.21
  24.5 0.0 copy-start.4
  24.6 1.8 collective-permute-start
  26.3 1.3 collective-permute-start.1
  27.6 4.9 %multiply_reduce_fusion.2 = (f32[512]{0:T(512)S(1)}, f32[512,128]{0,1:T(8,128)S(1)}) fusion(bf16[5376,128]{1,0:T(8,128)(2,1)} %param.10, f32[5376]{0:T(1024)S(1)} %copy-done.5, f32[512]{0:T(512)S(1)} %add_rsqrt_fusion.3, bf16[512,5376]{0,1:T(8,128)(2,1)} %copy.9), kind=kOutput, calls=%fused_computation.40 | convolution fusion | flops 715783680 | bytes 7169024 | tf_op jit(solution)/shard_map/dot_general | solution.py:74
  32.6 0.1 multiply_multiply_fusion.1
  32.7 0.0 collective-permute-done
  32.7 0.0 collective-permute-done.1
  32.8 9.1 %collective-permute-start.3 = (bf16[512,256]{0,1:T(8,128)(2,1)S(1)}, bf16[512,256]{0,1:T(8,128)(2,1)S(1)}, u32[]{:S(2)}, u32[]{:S(2)}) collective-permute-start(bf16[512,256]{0,1:T(8,128)(2,1)S(1)} %pad_maximum_fusion.2), channel_id=1, source_target_pairs={{0,24},{24,48},{48,72},{72,96},{96,120},{120,144},{144,168},{168,1... | collective-permute-start | bytes 786440 | tf_op jit(solution)/shard_map/ppermute | solution.py:34
  41.9 5.4 %collective-permute-start.2 = (bf16[512,256]{0,1:T(8,128)(2,1)S(1)}, bf16[512,256]{0,1:T(8,128)(2,1)S(1)}, u32[]{:S(2)}, u32[]{:S(2)}) collective-permute-start(bf16[512,256]{0,1:T(8,128)(2,1)S(1)} %pad_maximum_fusion.2), channel_id=1, source_target_pairs={{0,48},{24,72},{48,96},{72,120},{96,144},{120,168},{144,192},{168,... | collective-permute-start | bytes 786440 | tf_op jit(solution)/shard_map/ppermute | solution.py:34
  47.4 25.1 %collective-permute-done.3 = bf16[512,256]{0,1:T(8,128)(2,1)S(1)} collective-permute-done((bf16[512,256]{0,1:T(8,128)(2,1)S(1)}, bf16[512,256]{0,1:T(8,128)(2,1)S(1)}, u32[]{:S(2)}, u32[]{:S(2)}) %collective-permute-start.3) | collective-permute-done | bytes 262176 | tf_op jit(solution)/shard_map/ppermute | solution.py:34
  72.5 0.0 collective-permute-done.2
  72.5 0.1 maximum_maximum_fusion
  72.5 1.3 fusion.28
  73.9 1.7 copy-done.1
  75.5 0.6 fusion.2
  76.1 7.2 %convolution_convert_fusion = bf16[512,5376]{0,1:T(8,128)(2,1)} fusion(bf16[128,5376]{1,0:T(8,128)(2,1)S(1)} %copy-done, f32[512,1536]{1,0:T(8,128)} %copy-done.1, f32[512]{0:T(512)S(1)} %fusion.2, f32[512]{0:T(512)S(1)} %get-tuple-element.17, bf16[1536,256]{0,1:T(8,128)(2,1)S(1)} %maximum_maximum_fusion), kind=kOutput, calls=%fused_computation.2 | convolution fusion | flops 911147008 | bytes 10424320 | tf_op jit(solution)/shard_map/dot_general | solution.py:109
  83.3 0.0 reduce-scatter.2.cloned.1.call-update
  83.3 0.0 copy-start.3
  83.3 8.3 %convert_element_type.34 = f32[512,5376]{0,1:T(8,128)} convert(bf16[512,5376]{0,1:T(8,128)(2,1)} %copy.9) | non-fusion elementwise | flops 2752512 | bytes 16515072 | tf_op jit(solution)/shard_map/convert_element_type | solution.py:70
  91.6 129.8 %reduce-scatter.2.cloned.1.call-done = bf16[512,224]{0,1:T(8,128)(2,1)} async-done(((bf16[512,5376]{0,1:T(8,128)(2,1)}), bf16[512,224]{0,1:T(8,128)(2,1)}) %reduce-scatter.2.cloned.1.call-update) | async-done | bytes 229392 | tf_op jit(solution)/shard_map/reduce_scatter | solution.py:110
  221.4 1.0 fusion.7
  222.4 52.8 %psum.7 = f32[512]{0:T(512)S(1)} all-reduce(f32[512]{0:T(512)S(1)} %fusion.7), channel_id=1, replica_groups=mesh['ctx'=32,'tp'=24] {'tp'}, use_global_device_ids=true, to_apply=%region_7.8 | all-reduce | flops 512 | bytes 4096 | tf_op jit(solution)/shard_map/psum | solution.py:113
  275.2 1.9 fusion.10
  (19 shorter events, 0.1 us)
Async XLA Ops:
  6.5 69.6 %copy-start = (bf16[128,5376]{1,0:T(8,128)(2,1)S(1)}, bf16[128,5376]{1,0:T(8,128)(2,1)}, u32[]{:S(2)}) copy-start(bf16[128,5376]{1,0:T(8,128)(2,1)} %param.14) | copy-start | bytes 4128772
  6.5 214.8 %reduce-scatter.2.cloned.1.call-start = ((), (), s32[]{:S(2)}) async-start(), calls=%async_computation.1 | async-start | bytes 5734400 | tf_op jit(solution)/shard_map/reduce_scatter | solution.py:110
  15.0 3.8 %copy-start.5 = (f32[5376]{0:T(1024)S(1)}, f32[5376]{0:T(1024)}, u32[]{:S(2)}) copy-start(f32[5376]{0:T(1024)} %param.9) | copy-start | bytes 64516
  18.8 5.0 %copy-start.2 = (f32[128]{0:T(128)S(1)}, f32[128]{0:T(128)}, u32[]{:S(2)}) copy-start(f32[128]{0:T(128)} %param.13) | copy-start | bytes 1540
  24.5 8.0 %copy-start.4 = (f32[128]{0:T(128)S(1)}, f32[128]{0:T(128)}, u32[]{:S(2)}) copy-start(f32[128]{0:T(128)} %param.12) | copy-start | bytes 1540
  24.6 8.1 %collective-permute-start = (bf16[512,128]{0,1:T(8,128)(2,1)S(1)}, bf16[512,128]{0,1:T(8,128)(2,1)S(1)}, u32[]{:S(2)}, u32[]{:S(2)}) collective-permute-start(bf16[512,128]{0,1:T(8,128)(2,1)S(1)} %fusion.21), channel_id=1, source_target_pairs={{0,1},{1,2},{2,3},{3,4},{4,5},{5,6},{6,7},{7,8},{8,9},{9,10},{10,1... | collective-permute-start | bytes 393224 | tf_op jit(solution)/shard_map/ppermute | solution.py:22
  26.3 6.4 %collective-permute-start.1 = (bf16[512,128]{0,1:T(8,128)(2,1)S(1)}, bf16[512,128]{0,1:T(8,128)(2,1)S(1)}, u32[]{:S(2)}, u32[]{:S(2)}) collective-permute-start(bf16[512,128]{0,1:T(8,128)(2,1)S(1)} %fusion.21), channel_id=1, source_target_pairs={{1,0},{2,1},{3,2},{4,3},{5,4},{6,5},{7,6},{8,7},{9,8},{10,9},{11,1... | collective-permute-start | bytes 393224 | tf_op jit(solution)/shard_map/ppermute | solution.py:24
  32.8 39.7 %collective-permute-start.3 = (bf16[512,256]{0,1:T(8,128)(2,1)S(1)}, bf16[512,256]{0,1:T(8,128)(2,1)S(1)}, u32[]{:S(2)}, u32[]{:S(2)}) collective-permute-start(bf16[512,256]{0,1:T(8,128)(2,1)S(1)} %pad_maximum_fusion.2), channel_id=1, source_target_pairs={{0,24},{24,48},{48,72},{72,96},{96,120},{120,144},{144,168},{168,1... | collective-permute-start | bytes 786440 | tf_op jit(solution)/shard_map/ppermute | solution.py:34
  41.9 30.6 %collective-permute-start.2 = (bf16[512,256]{0,1:T(8,128)(2,1)S(1)}, bf16[512,256]{0,1:T(8,128)(2,1)S(1)}, u32[]{:S(2)}, u32[]{:S(2)}) collective-permute-start(bf16[512,256]{0,1:T(8,128)(2,1)S(1)} %pad_maximum_fusion.2), channel_id=1, source_target_pairs={{0,48},{24,72},{48,96},{72,120},{96,144},{120,168},{144,192},{168,... | collective-permute-start | bytes 786440 | tf_op jit(solution)/shard_map/ppermute | solution.py:34
  73.8 1.7 copy-start.1
  83.3 191.9 %copy-start.3 = (f32[224]{0:T(256)S(1)}, f32[224]{0:T(256)}, u32[]{:S(2)}) copy-start(f32[224]{0:T(256)} %param.15) | copy-start | bytes 2692
Sparse Core Ops, SparseCore 0:
  83.4 137.9 reduce-scatter.1
where the time goes:
time: 285 us; the launch traced here: 284 us
  waiting for transfers between devices  155 us (54%)
  blocking collectives  52.8 us (19%)
  matrix products  18.3 us (6%)
  starting transfers between devices  17.6 us (6%)
  other arithmetic  16.6 us (6%)
  between operations  13.6 us (5%)
  local copies, waits for them, and re-layouts  10.1 us (4%)
    reduce_scatter x1, waiting for transfers between devices, body(): lax.psum_scatter(partial_sum.astype(jnp.bfloat16), 'tp', scatter_dimensio...  130 us
    psum x1, blocking collectives, body(): squares = lax.psum(jnp.sum(summed * summed, axis=1), 'tp')  52.8 us
    ppermute x2, waiting for transfers between devices, from_behind(): return lax.ppermute(block, axis, route)  25.1 us
    ppermute x2, starting transfers between devices, from_behind(): return lax.ppermute(block, axis, route)  14.5 us
    unnamed x13, local copies, waits for them, and re-layouts  10.1 us
    convert_element_type x1, other arithmetic, body(): as_float = tokens.astype(jnp.float32)  8.32 us
    dot_general x1, matrix products, body(): jnp.dot(attended, out_weight, preferred_element_type=jnp.float32)  7.17 us
  transfers between devices with their start and end apart: 5, of which 2 were waited for; matrix products, arithmetic and copies ran while one was open for 5% of the time, Pallas kernels for 0%

commit v1 on v0

v1 whole, which is shorter than its diff:
```python
import jax
import jax.numpy as jnp
from jax import lax
from jax.sharding import Mesh, PartitionSpec as P

WIN = 1024


epsilon = 1e-06
query_scalar = 168.0
rope_base = 10000.0

TP_AXES = ("zl", "x", "core")


def from_behind(block, axis, distance):
    devices = range(lax.axis_size(axis))
    route = [(i - distance, i) for i in devices if i - distance in devices]
    return lax.ppermute(block, axis, route)


def rope_tables(positions, head_width):
    half_width = head_width // 2
    exponent = jnp.arange(half_width, dtype=jnp.float32) * (2.0 / head_width)
    frequency = rope_base ** (-exponent)
    angles = positions.astype(jnp.float32)[:, None] * frequency[None, :]
    cosine = jnp.concatenate([jnp.cos(angles), jnp.cos(angles)], axis=1)
    sine_table = jnp.concatenate([jnp.sin(angles), jnp.sin(angles)], axis=1)
    return (cosine, sine_table)


def rotate(signal, cosine, sine_table):
    half_width = signal.shape[-1] // 2
    turned = jnp.concatenate([-signal[:, half_width:], signal[:, :half_width]], axis=1)
    return signal * cosine + turned * sine_table


def rms_scale(signal, gain_vector):
    return (
        signal
        * lax.rsqrt(jnp.mean(signal * signal, axis=-1, keepdims=True) + epsilon)
        * gain_vector
    )


def body(
    tokens, norm_gain, query_weight, keyval_weight, query_gain, key_gain, out_weight, post_gain
):
    tok_rows = tokens.shape[0]
    model_width = tokens.shape[1]
    head_width = query_weight.shape[1]
    col_share = post_gain.shape[0]
    n_zl = lax.axis_size("zl")
    n_x = lax.axis_size("x")
    n_core = lax.axis_size("core")
    ctx_index = lax.axis_index("ctx")
    core_index = lax.axis_index("core")
    tp_index = (lax.axis_index("zl") * n_x + lax.axis_index("x")) * n_core + core_index
    is_even = core_index == 0

    as_float = tokens.astype(jnp.float32)
    normed = rms_scale(as_float, norm_gain).astype(jnp.bfloat16)
    positions = ctx_index * tok_rows + jnp.arange(tok_rows, dtype=jnp.int32)
    cosine, sine_table = rope_tables(positions, head_width)

    projected = jnp.dot(normed, keyval_weight, preferred_element_type=jnp.float32)
    rotated = rotate(rms_scale(projected, key_gain), cosine, sine_table)
    own_block = jnp.where(is_even, rotated, projected).astype(jnp.bfloat16)
    span_count = WIN // tok_rows
    earlier = [from_behind(own_block, "ctx", offset) for offset in range(span_count, 0, -1)]
    own_window = jnp.concatenate(earlier + [own_block], axis=0)
    other_window = lax.ppermute(own_window, "core", [(0, 1), (1, 0)])
    key_window = jnp.where(is_even, own_window, other_window)
    value_window = jnp.where(is_even, other_window, own_window)

    queries = jnp.dot(normed, query_weight, preferred_element_type=jnp.float32)
    queries = (
        rotate(rms_scale(queries, query_gain), cosine, sine_table) * query_scalar ** (-0.5)
    ).astype(jnp.bfloat16)

    key_pos = ctx_index * tok_rows - WIN + jnp.arange(WIN + tok_rows, dtype=jnp.int32)
    distance = positions[:, None] - key_pos[None, :]
    allowed = (key_pos[None, :] >= 0) & (distance >= 0) & (distance < WIN)
    scores = lax.dot_general(
        queries,
        key_window,
        (((1,), (1,)), ((), ())),
        preferred_element_type=jnp.float32,
    )
    scores = jnp.where(allowed, scores, -1e30)
    row_max = jnp.max(scores, axis=1, keepdims=True)
    lifted = jnp.exp(scores - row_max)
    weights = (lifted / jnp.sum(lifted, axis=1, keepdims=True)).astype(jnp.bfloat16)
    attended = jnp.dot(weights, value_window, preferred_element_type=jnp.float32).astype(
        jnp.bfloat16
    )

    permuted_weight = (
        out_weight.reshape(head_width, n_zl, n_x, n_core, col_share)
        .transpose(0, 3, 2, 1, 4)
        .reshape(head_width, model_width)
    )
    partial_sum = lax.dot_general(
        permuted_weight,
        attended,
        (((0,), (1,)), ((), ())),
        preferred_element_type=jnp.float32,
    )
    reduced = partial_sum.astype(jnp.bfloat16)
    for axis in ("core", "x", "zl"):
        reduced = lax.psum_scatter(reduced, axis, scatter_dimension=0, tiled=True)
    summed = reduced.astype(jnp.float32).T
    squares = jnp.sum(summed * summed, axis=1)
    for axis in ("core", "x", "zl"):
        squares = lax.psum(squares, axis)
    scaled = summed * lax.rsqrt(squares[:, None] / model_width + epsilon) * post_gain
    residual = lax.dynamic_slice_in_dim(tokens, tp_index * col_share, col_share, 1)
    return (residual.astype(jnp.float32) + scaled).astype(jnp.bfloat16)


def solution(mesh):
    n_ctx, n_tp = mesh.devices.shape
    n_core = 2
    n_x = 4
    n_zl = n_tp // (n_core * n_x)
    fine = Mesh(mesh.devices.reshape(n_ctx, n_zl, n_x, n_core), ("ctx",) + TP_AXES)
    return jax.shard_map(
        body,
        mesh=fine,
        in_specs=(
            P("ctx", None),
            P(),
            P(None, TP_AXES),
            P(None, TP_AXES),
            P(),
            P(),
            P(TP_AXES, None),
            P(TP_AXES),
        ),
        out_specs=P("ctx", TP_AXES),
        check_vma=False,
    )
```

time: 285 us -> 209 us (0.73)
  the two profiles are of different devices: /device:TPU:208 before, /device:TPU:56 now
where the time goes in v1:
time: 209 us; the launch traced here: 208 us
  waiting for transfers between devices  112 us (54%)
  starting transfers between devices  22.9 us (11%)
  blocking collectives  18.7 us (9%)
  matrix products  18.1 us (9%)
  local copies, waits for them, and re-layouts  15 us (7%)
  between operations  13.4 us (6%)
  other arithmetic  7.48 us (4%)
    unnamed x6, waiting for transfers between devices  101 us
    ppermute x2, starting transfers between devices, from_behind(): return lax.ppermute(block, axis, route)  20.9 us
    psum x3, blocking collectives, body(): squares = lax.psum(squares, axis)  18.7 us
    unnamed x23, local copies, waits for them, and re-layouts  13 us
    ppermute x2, waiting for transfers between devices, from_behind(): return lax.ppermute(block, axis, route)  11 us
    dot_general x1, matrix products, body(): lax.dot_general(permuted_weight, attended, (((0,), (1,)), ((), ())), pref...  7.03 us
    dot_general x1, matrix products, body(): queries = jnp.dot(normed, query_weight, preferred_element_type=jnp.float32)  5.03 us
    dot_general x1, matrix products, body(): jnp.dot(normed, keyval_weight, preferred_element_type=jnp.float32)  4.63 us
  transfers between devices with their start and end apart: 6, of which 4 were waited for; matrix products, arithmetic and copies ran while one was open for 4% of the time, Pallas kernels for 0%

profile of v1, /device:TPU:56, one launch (start us, length us, event | category | flops | bytes accessed | tf_op | source)
XLA Modules:
  0.0 207.9 jit_solution(11949914281303795551)
XLA Ops:
  6.6 3.8 %fusion = f32[512]{0:T(512)S(1)} fusion(bf16[512,5376]{1,0:T(8,128)(2,1)} %param.8), kind=kLoop, calls=%fused_computation.2 | loop fusion | flops 8257024 | bytes 5507072 | tf_op jit(solution)/shard_map/reduce_sum | solution.py:41
  10.4 4.6 %multiply_reduce_fusion = (f32[512]{0:T(512)S(1)}, f32[512,128]{0,1:T(8,128)S(1)}) fusion(bf16[5376,128]{1,0:T(8,128)(2,1)S(1)} %copy-done, bf16[512,5376]{1,0:T(8,128)(2,1)} %param.8, f32[5376]{0:T(1024)S(1)} %copy-done.9, f32[512]{0:T(512)S(1)} %add_rsqrt_fusion.3), kind=kOutput, calls=%fused_computation.44 | convolution fusion | flops 715783680 | bytes 7169024 | tf_op jit(solution)/shard_map/dot_general | solution.py:66
  15.1 0.1 multiply_multiply_fusion
  15.2 0.5 multiply_sine_fusion
  15.7 0.1 fusion.31
  15.9 7.9 %collective-permute-start.1 = (bf16[512,128]{0,1:T(8,128)(2,1)S(1)}, bf16[512,128]{0,1:T(8,128)(2,1)S(1)}, u32[]{:S(2)}, u32[]{:S(2)}) collective-permute-start(bf16[512,128]{0,1:T(8,128)(2,1)S(1)} %fusion.31), channel_id=1, source_target_pairs={{0,24},{24,48},{48,72},{72,96},{96,120},{120,144},{144,168},{168,1... | collective-permute-start | bytes 393224 | tf_op jit(solution)/shard_map/ppermute | solution.py:19
  23.8 13.0 %collective-permute-start = (bf16[512,128]{0,1:T(8,128)(2,1)S(1)}, bf16[512,128]{0,1:T(8,128)(2,1)S(1)}, u32[]{:S(2)}, u32[]{:S(2)}) collective-permute-start(bf16[512,128]{0,1:T(8,128)(2,1)S(1)} %fusion.31), channel_id=1, source_target_pairs={{0,48},{24,72},{48,96},{72,120},{96,144},{120,168},{144,192},{168,... | collective-permute-start | bytes 393224 | tf_op jit(solution)/shard_map/ppermute | solution.py:19
  36.8 5.0 %multiply_reduce_fusion.1 = (f32[512]{0:T(512)S(1)}, f32[512,128]{0,1:T(8,128)S(1)}) fusion(bf16[5376,128]{1,0:T(8,128)(2,1)} %param.10, bf16[512,5376]{1,0:T(8,128)(2,1)} %param.8, f32[5376]{0:T(1024)S(1)} %copy-done.9, f32[512]{0:T(512)S(1)} %add_rsqrt_fusion.3), kind=kOutput, calls=%fused_computation.46 | convolution fusion | flops 715783680 | bytes 7169024 | tf_op jit(solution)/shard_map/dot_general | solution.py:76
  41.9 0.1 multiply_multiply_fusion.1
  42.0 11.0 %collective-permute-done = bf16[512,128]{0,1:T(8,128)(2,1)S(1)} collective-permute-done((bf16[512,128]{0,1:T(8,128)(2,1)S(1)}, bf16[512,128]{0,1:T(8,128)(2,1)S(1)}, u32[]{:S(2)}, u32[]{:S(2)}) %collective-permute-start) | collective-permute-done | bytes 131104 | tf_op jit(solution)/shard_map/ppermute | solution.py:19
  53.0 0.8 pad_maximum_fusion
  53.8 1.9 collective-permute-start.2
  55.7 1.8 copy.13
  57.5 1.2 copy.14
  58.8 1.4 fusion.38
  60.2 1.6 copy-done.1
  61.8 0.6 fusion.6
  62.4 0.1 copy-done.2
  62.5 0.1 copy-done.5
  62.6 7.0 %fusion.3 = bf16[5376,512]{0,1:T(8,128)(2,1)} fusion(bf16[128,5376]{0,1:T(8,128)(2,1)S(1)} %bitcast.19, f32[512,1536]{1,0:T(8,128)} %copy-done.1, f32[512]{0:T(512)S(1)} %fusion.6, f32[512]{0:T(512)S(1)} %get-tuple-element.15, bf16[1536,128]{0,1:T(8,128)(2,1)} %collective-permute-done.2, pred[]{:T(512)S(6)} %eq.3, bf16[512,128]{0,1:T(8,128)(2,1)S(1)} %fusion.31, ...), kind=kOutput, calls=%fused_computation.6 | convolution fusion | flops 912523264 | bytes 10817537 | tf_op jit(solution)/shard_map/dot_general | solution.py:103
  69.6 8.3 %copy.16 = bf16[5376,512]{1,0:T(8,128)(2,1)} copy(bf16[5376,512]{0,1:T(8,128)(2,1)} %fusion.3) | data formatting | bytes 11010048
  77.9 0.0 reduce-scatter.12.cloned.1.call-start
  78.0 20.5 %reduce-scatter.10.cloned.1.call-done = bf16[2688,512]{1,0:T(8,128)(2,1)} async-done(((bf16[5376,512]{1,0:T(8,128)(2,1)}), bf16[2688,512]{1,0:T(8,128)(2,1)}) %reduce-scatter.10.cloned.1.call-update) | async-done | bytes 2752528
  98.5 47.6 %reduce-scatter.12.cloned.1.call-done = bf16[672,512]{1,0:T(8,128)(2,1)} async-done(((bf16[2688,512]{1,0:T(8,128)(2,1)}), bf16[672,512]{1,0:T(8,128)(2,1)}) %reduce-scatter.12.cloned.1.call-update) | async-done | bytes 688144
  146.1 33.3 %reduce-scatter.14.cloned.1.call-done = bf16[224,512]{1,0:T(8,128)(2,1)} async-done(((bf16[672,512]{1,0:T(8,128)(2,1)}), bf16[224,512]{1,0:T(8,128)(2,1)}) %reduce-scatter.14.cloned.1.call-update) | async-done | bytes 229392
  179.4 1.1 copy.21
  180.5 0.1 fusion.13
  180.7 2.5 %psum.21 = f32[512]{0:T(512)S(1)} all-reduce(f32[512]{0:T(512)S(1)} %fusion.13), channel_id=1, replica_groups=mesh['ctx'=32,'zl'=3,'x'=4,'core'=2] {'core'}, use_global_device_ids=true, to_apply=%region_9.10 | all-reduce | flops 512 | bytes 4096 | tf_op jit(solution)/shard_map/psum | solution.py:115
  183.1 10.4 %psum.22 = f32[512]{0:T(512)S(1)} all-reduce(f32[512]{0:T(512)S(1)} %psum.21), channel_id=1, replica_groups=mesh['ctx'=32,'zl'=3,'x'=4,'core'=2] {'x'}, use_global_device_ids=true, to_apply=%region_10.11 | all-reduce | flops 512 | bytes 4096 | tf_op jit(solution)/shard_map/psum | solution.py:115
  193.5 5.8 %psum.23 = f32[512]{0:T(512)S(1)} all-reduce(f32[512]{0:T(512)S(1)} %psum.22), channel_id=1, replica_groups=mesh['ctx'=32,'zl'=3,'x'=4,'core'=2] {'zl'}, use_global_device_ids=true, to_apply=%region_11.12 | all-reduce | flops 512 | bytes 4096 | tf_op jit(solution)/shard_map/psum | solution.py:115
  199.3 1.2 fusion.17
  200.6 0.8 copy.15
  (34 shorter events, 0.2 us)
Async XLA Ops:
  6.5 3.9 %copy-start = (bf16[5376,128]{1,0:T(8,128)(2,1)S(1)}, bf16[5376,128]{1,0:T(8,128)(2,1)}, u32[]{:S(2)}) copy-start(bf16[5376,128]{1,0:T(8,128)(2,1)} %param.11) | copy-start | bytes 4128772
  6.5 3.9 %copy-start.9 = (f32[5376]{0:T(1024)S(1)}, f32[5376]{0:T(1024)}, u32[]{:S(2)}) copy-start(f32[5376]{0:T(1024)} %param.9) | copy-start | bytes 64516
  6.5 91.9 %reduce-scatter.10.cloned.1.call-start = ((), (), s32[]{:S(2)}) async-start(), calls=%async_computation.3 | async-start | bytes 8257536
  10.4 4.7 %copy-start.6 = (f32[128]{0:T(128)S(1)}, f32[128]{0:T(128)}, u32[]{:S(2)}) copy-start(f32[128]{0:T(128)} %param.13) | copy-start | bytes 1540
  15.8 26.0 %copy-start.8 = (f32[128]{0:T(128)S(1)}, f32[128]{0:T(128)}, u32[]{:S(2)}) copy-start(f32[128]{0:T(128)} %param.12) | copy-start | bytes 1540
  15.9 26.1 %collective-permute-start.1 = (bf16[512,128]{0,1:T(8,128)(2,1)S(1)}, bf16[512,128]{0,1:T(8,128)(2,1)S(1)}, u32[]{:S(2)}, u32[]{:S(2)}) collective-permute-start(bf16[512,128]{0,1:T(8,128)(2,1)S(1)} %fusion.31), channel_id=1, source_target_pairs={{0,24},{24,48},{48,72},{72,96},{96,120},{120,144},{144,168},{168,1... | collective-permute-start | bytes 393224 | tf_op jit(solution)/shard_map/ppermute | solution.py:19
  23.8 29.2 %collective-permute-start = (bf16[512,128]{0,1:T(8,128)(2,1)S(1)}, bf16[512,128]{0,1:T(8,128)(2,1)S(1)}, u32[]{:S(2)}, u32[]{:S(2)}) collective-permute-start(bf16[512,128]{0,1:T(8,128)(2,1)S(1)} %fusion.31), channel_id=1, source_target_pairs={{0,48},{24,72},{48,96},{72,120},{96,144},{120,168},{144,192},{168,... | collective-permute-start | bytes 393224 | tf_op jit(solution)/shard_map/ppermute | solution.py:19
  53.0 2.7 %copy-start.3 = (bf16[512,128]{0,1:T(8,128)(2,1)}, bf16[512,128]{0,1:T(8,128)(2,1)S(1)}, u32[]{:S(2)}) copy-start(bf16[512,128]{0,1:T(8,128)(2,1)S(1)} %collective-permute-done) | copy-start | bytes 393220
  53.8 5.0 %collective-permute-start.2 = (bf16[1536,128]{0,1:T(8,128)(2,1)}, bf16[1536,128]{0,1:T(8,128)(2,1)}, u32[]{:S(2)}, u32[]{:S(2)}) collective-permute-start(bf16[1536,128]{0,1:T(8,128)(2,1)} %pad_maximum_fusion), channel_id=1, source_target_pairs={{0,1},{1,0},{2,3},{3,2},{4,5},{5,4},{6,7},{7,6},{8,9},{9,8},{10,11... | collective-permute-start | bytes 1179656 | tf_op jit(solution)/shard_map/ppermute | solution.py:72
  57.5 1.2 copy-start.4
  60.1 1.7 copy-start.1
  60.2 2.3 %copy-start.2 = (bf16[128,2,4,3,224]{0,4,3,2,1:T(8,128)(2,1)S(1)}, bf16[128,2,4,3,224]{0,4,3,2,1:T(8,128)(2,1)}, u32[]{:S(2)}) copy-start(bf16[128,2,4,3,224]{0,4,3,2,1:T(8,128)(2,1)} %copy.14) | copy-start | bytes 4128772
  60.2 2.4 %copy-start.5 = (bf16[512,128]{0,1:T(8,128)(2,1)S(1)}, bf16[512,128]{0,1:T(8,128)(2,1)}, u32[]{:S(2)}) copy-start(bf16[512,128]{0,1:T(8,128)(2,1)} %copy-done.3) | copy-start | bytes 393220
  77.9 121.5 %copy-start.7 = (f32[224]{0:T(256)S(1)}, f32[224]{0:T(256)}, u32[]{:S(2)}) copy-start(f32[224]{0:T(256)} %param.15) | copy-start | bytes 2692
  77.9 68.2 %reduce-scatter.12.cloned.1.call-start = ((), (), s32[]{:S(2)}) async-start(), calls=%async_computation.4 | async-start | bytes 3440640
  98.4 81.0 %reduce-scatter.14.cloned.1.call-start = ((), (), s32[]{:S(2)}) async-start(), calls=%async_computation.5 | async-start | bytes 917504
Sparse Core Ops, SparseCore 0:
  78.0 20.3 reduce-scatter.9
  101.6 44.4 reduce-scatter.11
  149.3 30.1 reduce-scatter.13

commit v2 on v1

--- a/solution.py
+++ b/solution.py
@@ -95,21 +95,11 @@
         jnp.bfloat16
     )
 
-    permuted_weight = (
-        out_weight.reshape(head_width, n_zl, n_x, n_core, col_share)
-        .transpose(0, 3, 2, 1, 4)
-        .reshape(head_width, model_width)
-    )
-    partial_sum = lax.dot_general(
-        permuted_weight,
-        attended,
-        (((0,), (1,)), ((), ())),
-        preferred_element_type=jnp.float32,
-    )
-    reduced = partial_sum.astype(jnp.bfloat16)
-    for axis in ("core", "x", "zl"):
-        reduced = lax.psum_scatter(reduced, axis, scatter_dimension=0, tiled=True)
-    summed = reduced.astype(jnp.float32).T
+    partial_sum = jnp.dot(attended, out_weight, preferred_element_type=jnp.float32)
+    n_tp = n_zl * n_x * n_core
+    pieces = partial_sum.astype(jnp.bfloat16).reshape(tok_rows, n_tp, col_share)
+    received = lax.all_to_all(pieces, TP_AXES, 1, 1, tiled=True)
+    summed = jnp.sum(received.astype(jnp.float32), axis=1)
     squares = jnp.sum(summed * summed, axis=1)
     for axis in ("core", "x", "zl"):
         squares = lax.psum(squares, axis)

time: 209 us -> 178 us (0.85)
  waiting for transfers between devices: 112 us -> 88.5 us
  between operations: 13.4 us -> 0.23 us
  starting transfers between devices: 22.9 us -> 30.1 us
  local copies, waits for them, and re-layouts: 15 us -> 11.6 us
  other arithmetic: 7.48 us -> 9.64 us
    unnamed x6 -> x0, waiting for transfers between devices: 101 us -> none
    all_to_all x0 -> x1, waiting for transfers between devices: none -> 80.4 us  [body(): received = lax.all_to_all(pieces, TP_AXES, 1, 1, tiled=True)]
    unnamed x23 -> x15, local copies, waits for them, and re-layouts: 13 us -> 2.21 us
    all_to_all x0 -> x1, starting transfers between devices: none -> 7.86 us  [body(): received = lax.all_to_all(pieces, TP_AXES, 1, 1, tiled=True)]
    convert_element_type x1, local copies, waits for them, and re-layouts: 0.82 us -> 8.27 us  [body(): pieces = partial_sum.astype(jnp.bfloat16).reshape(tok_rows, n_tp, col_share)]
    ppermute x2, waiting for transfers between devices: 11 us -> 6.51 us  [from_behind(): return lax.ppermute(block, axis, route)]
    reduce_sum x0 -> x1, other arithmetic: none -> 3.39 us  [body(): summed = jnp.sum(received.astype(jnp.float32), axis=1)]
  transfers between devices with their start and end apart: 6 -> 4, of which waited for: 4 -> 3; matrix products, arithmetic and copies ran while one was open for 4% -> 4% of each run, Pallas kernels for 0% -> 0%
where the time goes in v2:
time: 178 us; the launch traced here: 177 us
  waiting for transfers between devices  88.5 us (50%)
  starting transfers between devices  30.1 us (17%)
  blocking collectives  20.1 us (11%)
  matrix products  17.1 us (10%)
  local copies, waits for them, and re-layouts  11.6 us (7%)
  other arithmetic  9.64 us (5%)
    all_to_all x1, waiting for transfers between devices, body(): received = lax.all_to_all(pieces, TP_AXES, 1, 1, tiled=True)  80.4 us
    ppermute x2, starting transfers between devices, from_behind(): return lax.ppermute(block, axis, route)  20.3 us
    psum x3, blocking collectives, body(): squares = lax.psum(squares, axis)  20.1 us
    convert_element_type x1, local copies, waits for them, and re-layouts, body(): pieces = partial_sum.astype(jnp.bfloat16).reshape(tok_rows, n_tp, col_share)  8.27 us
    all_to_all x1, starting transfers between devices, body(): received = lax.all_to_all(pieces, TP_AXES, 1, 1, tiled=True)  7.86 us
    dot_general x1, matrix products, body(): jnp.dot(attended, out_weight, preferred_element_type=jnp.float32)  7.18 us
    ppermute x2, waiting for transfers between devices, from_behind(): return lax.ppermute(block, axis, route)  6.51 us
    dot_general x1, matrix products, body(): queries = jnp.dot(normed, query_weight, preferred_element_type=jnp.float32)  5.03 us
  transfers between devices with their start and end apart: 4, of which 3 were waited for; matrix products, arithmetic and copies ran while one was open for 4% of the time, Pallas kernels for 0%

profile of v2, /device:TPU:56, one launch (start us, length us, event | category | flops | bytes accessed | tf_op | source)
XLA Modules:
  0.0 177.3 jit_solution(3032494932845529930)
XLA Ops:
  0.0 3.9 %fusion = f32[512]{0:T(512)S(1)} fusion(bf16[512,5376]{1,0:T(8,128)(2,1)} %param.8), kind=kLoop, calls=%fused_computation.2 | loop fusion | flops 8257024 | bytes 5507072 | tf_op jit(solution)/shard_map/reduce_sum | solution.py:41
  3.9 0.4 copy-done.1
  4.3 3.5 %multiply_reduce_fusion.1 = (f32[512]{0:T(512)S(1)}, f32[512,128]{0,1:T(8,128)S(1)}) fusion(bf16[5376,128]{1,0:T(8,128)(2,1)} %param.11, bf16[512,5376]{1,0:T(8,128)(2,1)S(1)} %copy-done.1, f32[5376]{0:T(1024)} %param.9, f32[512]{0:T(512)S(1)} %add_rsqrt_fusion.3), kind=kOutput, calls=%fused_computation.39 | convolution fusion | flops 715783680 | bytes 7169024 | tf_op jit(solution)/shard_map/dot_general | solution.py:66
  7.8 0.1 multiply_multiply_fusion
  7.9 0.5 multiply_sine_fusion
  8.5 0.1 fusion.25
  8.6 0.0 copy-start.5
  8.6 15.1 %collective-permute-start = (bf16[512,128]{0,1:T(8,128)(2,1)S(1)}, bf16[512,128]{0,1:T(8,128)(2,1)S(1)}, u32[]{:S(2)}, u32[]{:S(2)}) collective-permute-start(bf16[512,128]{0,1:T(8,128)(2,1)S(1)} %fusion.25), channel_id=1, source_target_pairs={{0,48},{24,72},{48,96},{72,120},{96,144},{120,168},{144,192},{168,... | collective-permute-start | bytes 393224 | tf_op jit(solution)/shard_map/ppermute | solution.py:19
  23.7 5.2 %collective-permute-start.1 = (bf16[512,128]{0,1:T(8,128)(2,1)S(1)}, bf16[512,128]{0,1:T(8,128)(2,1)S(1)}, u32[]{:S(2)}, u32[]{:S(2)}) collective-permute-start(bf16[512,128]{0,1:T(8,128)(2,1)S(1)} %fusion.25), channel_id=1, source_target_pairs={{0,24},{24,48},{48,72},{72,96},{96,120},{120,144},{144,168},{168,1... | collective-permute-start | bytes 393224 | tf_op jit(solution)/shard_map/ppermute | solution.py:19
  29.0 5.0 %multiply_reduce_fusion.2 = (f32[512]{0:T(512)S(1)}, f32[512,128]{0,1:T(8,128)S(1)}) fusion(bf16[5376,128]{1,0:T(8,128)(2,1)} %param.10, bf16[512,5376]{1,0:T(8,128)(2,1)} %param.8, f32[5376]{0:T(1024)S(1)} %copy-done.6, f32[512]{0:T(512)S(1)} %add_rsqrt_fusion.3), kind=kOutput, calls=%fused_computation.41 | convolution fusion | flops 715783680 | bytes 7169024 | tf_op jit(solution)/shard_map/dot_general | solution.py:76
  34.0 0.0 copy-done.5
  34.0 0.1 multiply_multiply_fusion.1
  34.1 0.0 collective-permute-done
  34.1 6.5 %collective-permute-done.1 = bf16[512,128]{0,1:T(8,128)(2,1)S(1)} collective-permute-done((bf16[512,128]{0,1:T(8,128)(2,1)S(1)}, bf16[512,128]{0,1:T(8,128)(2,1)S(1)}, u32[]{:S(2)}, u32[]{:S(2)}) %collective-permute-start.1) | collective-permute-done | bytes 131104 | tf_op jit(solution)/shard_map/ppermute | solution.py:19
  40.7 1.9 %collective-permute-start.2 = (bf16[1536,128]{0,1:T(8,128)(2,1)S(1)}, bf16[1536,128]{0,1:T(8,128)(2,1)S(1)}, u32[]{:S(2)}, u32[]{:S(2)}) collective-permute-start(bf16[1536,128]{0,1:T(8,128)(2,1)S(1)} %pad_maximum_fusion), channel_id=1, source_target_pairs={{0,1},{1,0},{2,3},{3,2},{4,5},{5,4},{6,7},{7,6},{8,9},{9,8},{10,11... | collective-permute-start | bytes 1179656 | tf_op jit(solution)/shard_map/ppermute | solution.py:72
  42.7 1.6 collective-permute-done.2
  44.3 1.4 fusion.32
  45.7 1.7 copy-done.2
  47.3 0.6 fusion.5
  47.9 7.2 %convolution_convert_fusion = bf16[512,5376]{1,0:T(8,128)(2,1)} fusion(bf16[128,5376]{1,0:T(8,128)(2,1)S(1)} %copy-done, f32[512,1536]{1,0:T(8,128)} %copy-done.2, f32[512]{0:T(512)S(1)} %fusion.5, f32[512]{0:T(512)S(1)} %get-tuple-element.15, bf16[1536,128]{0,1:T(8,128)(2,1)S(1)} %collective-permute-done.2, pred[]{:T(512)S(6)} %eq.3, ...), kind=kOutput, calls=%fused_computation.6 | convolution fusion | flops 912523264 | bytes 10817537 | tf_op jit(solution)/shard_map/dot_general | solution.py:98
  55.1 8.3 %copy.11 = bf16[512,5376]{0,1:T(8,128)(2,1)} copy(bf16[512,5376]{1,0:T(8,128)(2,1)} %convolution_convert_fusion) | data formatting | bytes 11010048 | tf_op jit(solution)/shard_map/convert_element_type | solution.py:100
  63.4 7.9 %all-to-all-start = ((bf16[512,24,224]{0,2,1:T(8,128)(2,1)}), bf16[512,24,224]{0,2,1:T(8,128)(2,1)}, u32[]{:S(2)}, u32[]{:S(2)}) async-start(bf16[512,24,224]{0,2,1:T(8,128)(2,1)} %bitcast.4), calls=%async_computation | async-start | bytes 11010048 | tf_op jit(solution)/shard_map/all_to_all | solution.py:101
  71.2 1.1 constant_dynamic-slice_fusion
  72.4 0.1 copy.12
  72.5 0.0 copy-start.4
  72.5 80.4 %all-to-all-done = bf16[512,24,224]{0,2,1:T(8,128)(2,1)} async-done(((bf16[512,24,224]{0,2,1:T(8,128)(2,1)}), bf16[512,24,224]{0,2,1:T(8,128)(2,1)}, u32[]{:S(2)}, u32[]{:S(2)}) %all-to-all-start) | async-done | bytes 5505056 | tf_op jit(solution)/shard_map/all_to_all | solution.py:101
  152.9 3.4 %convert_reduce_fusion = f32[512,224]{0,1:T(8,128)S(1)} fusion(bf16[512,24,224]{0,2,1:T(8,128)(2,1)} %all-to-all-done), kind=kLoop, calls=%fused_computation.5 | loop fusion | flops 5390336 | bytes 5963776 | tf_op jit(solution)/shard_map/reduce_sum | solution.py:102
  156.3 0.1 multiply_reduce_fusion
  156.4 3.0 %psum.21 = f32[512]{0:T(512)S(1)} all-reduce(f32[512]{0:T(512)S(1)} %multiply_reduce_fusion), channel_id=1, replica_groups=mesh['ctx'=32,'zl'=3,'x'=4,'core'=2] {'core'}, use_global_device_ids=true, to_apply=%region_7.8 | all-reduce | flops 512 | bytes 4096 | tf_op jit(solution)/shard_map/psum | solution.py:105
  159.3 11.3 %psum.22 = f32[512]{0:T(512)S(1)} all-reduce(f32[512]{0:T(512)S(1)} %psum.21), channel_id=1, replica_groups=mesh['ctx'=32,'zl'=3,'x'=4,'core'=2] {'x'}, use_global_device_ids=true, to_apply=%region_8.9 | all-reduce | flops 512 | bytes 4096 | tf_op jit(solution)/shard_map/psum | solution.py:105
  170.6 5.8 %psum.23 = f32[512]{0:T(512)S(1)} all-reduce(f32[512]{0:T(512)S(1)} %psum.22), channel_id=1, replica_groups=mesh['ctx'=32,'zl'=3,'x'=4,'core'=2] {'zl'}, use_global_device_ids=true, to_apply=%region_9.10 | all-reduce | flops 512 | bytes 4096 | tf_op jit(solution)/shard_map/psum | solution.py:105
  176.5 0.8 add_convert_fusion
  (20 shorter events, 0.1 us)
Async XLA Ops:
  0.0 47.9 %copy-start = (bf16[128,5376]{1,0:T(8,128)(2,1)S(1)}, bf16[128,5376]{1,0:T(8,128)(2,1)}, u32[]{:S(2)}) copy-start(bf16[128,5376]{1,0:T(8,128)(2,1)} %param.14) | copy-start | bytes 4128772
  0.0 4.3 %copy-start.1 = (bf16[512,5376]{1,0:T(8,128)(2,1)S(1)}, bf16[512,5376]{1,0:T(8,128)(2,1)}, u32[]{:S(2)}) copy-start(bf16[512,5376]{1,0:T(8,128)(2,1)} %param.8) | copy-start | bytes 16515076
  4.3 3.5 %copy-start.3 = (f32[128]{0:T(128)S(1)}, f32[128]{0:T(128)}, u32[]{:S(2)}) copy-start(f32[128]{0:T(128)} %param.13) | copy-start | bytes 1540
  4.3 24.7 %copy-start.6 = (f32[5376]{0:T(1024)S(1)}, f32[5376]{0:T(1024)}, u32[]{:S(2)}) copy-start(f32[5376]{0:T(1024)} %param.9) | copy-start | bytes 64516
  8.6 25.4 %copy-start.5 = (f32[128]{0:T(128)S(1)}, f32[128]{0:T(128)}, u32[]{:S(2)}) copy-start(f32[128]{0:T(128)} %param.12) | copy-start | bytes 1540
  8.6 25.5 %collective-permute-start = (bf16[512,128]{0,1:T(8,128)(2,1)S(1)}, bf16[512,128]{0,1:T(8,128)(2,1)S(1)}, u32[]{:S(2)}, u32[]{:S(2)}) collective-permute-start(bf16[512,128]{0,1:T(8,128)(2,1)S(1)} %fusion.25), channel_id=1, source_target_pairs={{0,48},{24,72},{48,96},{72,120},{96,144},{120,168},{144,192},{168,... | collective-permute-start | bytes 393224 | tf_op jit(solution)/shard_map/ppermute | solution.py:19
  23.7 16.9 %collective-permute-start.1 = (bf16[512,128]{0,1:T(8,128)(2,1)S(1)}, bf16[512,128]{0,1:T(8,128)(2,1)S(1)}, u32[]{:S(2)}, u32[]{:S(2)}) collective-permute-start(bf16[512,128]{0,1:T(8,128)(2,1)S(1)} %fusion.25), channel_id=1, source_target_pairs={{0,24},{24,48},{48,72},{72,96},{96,120},{120,144},{144,168},{168,1... | collective-permute-start | bytes 393224 | tf_op jit(solution)/shard_map/ppermute | solution.py:19
  40.7 3.6 %collective-permute-start.2 = (bf16[1536,128]{0,1:T(8,128)(2,1)S(1)}, bf16[1536,128]{0,1:T(8,128)(2,1)S(1)}, u32[]{:S(2)}, u32[]{:S(2)}) collective-permute-start(bf16[1536,128]{0,1:T(8,128)(2,1)S(1)} %pad_maximum_fusion), channel_id=1, source_target_pairs={{0,1},{1,0},{2,3},{3,2},{4,5},{5,4},{6,7},{7,6},{8,9},{9,8},{10,11... | collective-permute-start | bytes 1179656 | tf_op jit(solution)/shard_map/ppermute | solution.py:72
  45.7 1.7 copy-start.2
  63.4 89.6 %all-to-all-start = ((bf16[512,24,224]{0,2,1:T(8,128)(2,1)}), bf16[512,24,224]{0,2,1:T(8,128)(2,1)}, u32[]{:S(2)}, u32[]{:S(2)}) async-start(bf16[512,24,224]{0,2,1:T(8,128)(2,1)} %bitcast.4), calls=%async_computation | async-start | bytes 11010048 | tf_op jit(solution)/shard_map/all_to_all | solution.py:101
  72.5 103.9 %copy-start.4 = (f32[224]{0:T(256)S(1)}, f32[224]{0:T(256)}, u32[]{:S(2)}) copy-start(f32[224]{0:T(256)} %param.15) | copy-start | bytes 2692

commit v3 on v2

--- a/solution.py
+++ b/solution.py
@@ -43,7 +43,7 @@
     )
 
 
-def body(
+def layer(
     tokens, norm_gain, query_weight, keyval_weight, query_gain, key_gain, out_weight, post_gain
 ):
     tok_rows = tokens.shape[0]
@@ -66,10 +66,17 @@
     projected = jnp.dot(normed, keyval_weight, preferred_element_type=jnp.float32)
     rotated = rotate(rms_scale(projected, key_gain), cosine, sine_table)
     own_block = jnp.where(is_even, rotated, projected).astype(jnp.bfloat16)
+    n_tp = n_zl * n_x * n_core
+    weight_block = lax.all_to_all(
+        out_weight.reshape(head_width, n_tp, col_share), TP_AXES, 1, 0, tiled=True
+    ).reshape(n_tp * head_width, col_share)
     span_count = WIN // tok_rows
     earlier = [from_behind(own_block, "ctx", offset) for offset in range(span_count, 0, -1)]
     own_window = jnp.concatenate(earlier + [own_block], axis=0)
     other_window = lax.ppermute(own_window, "core", [(0, 1), (1, 0)])
+    weight_block, own_window, other_window = lax.optimization_barrier(
+        (weight_block, own_window, other_window)
+    )
     key_window = jnp.where(is_even, own_window, other_window)
     value_window = jnp.where(is_even, other_window, own_window)
 
@@ -95,11 +102,8 @@
         jnp.bfloat16
     )
 
-    partial_sum = jnp.dot(attended, out_weight, preferred_element_type=jnp.float32)
-    n_tp = n_zl * n_x * n_core
-    pieces = partial_sum.astype(jnp.bfloat16).reshape(tok_rows, n_tp, col_share)
-    received = lax.all_to_all(pieces, TP_AXES, 1, 1, tiled=True)
-    summed = jnp.sum(received.astype(jnp.float32), axis=1)
+    all_heads = lax.all_gather(attended, TP_AXES, axis=1, tiled=True)
+    summed = jnp.dot(all_heads, weight_block, preferred_element_type=jnp.float32)
     squares = jnp.sum(summed * summed, axis=1)
     for axis in ("core", "x", "zl"):
         squares = lax.psum(squares, axis)
@@ -115,7 +119,7 @@
     n_zl = n_tp // (n_core * n_x)
     fine = Mesh(mesh.devices.reshape(n_ctx, n_zl, n_x, n_core), ("ctx",) + TP_AXES)
     return jax.shard_map(
-        body,
+        layer,
         mesh=fine,
         in_specs=(
             P("ctx", None),

time: 178 us -> 203 us (1.14)
  the two profiles are of different devices: /device:TPU:56 before, /device:TPU:192 now
where the time goes in v3:
time: 203 us; the launch traced here: 202 us
  waiting for transfers between devices  115 us (57%)
  starting transfers between devices  22.7 us (11%)
  blocking collectives  20.6 us (10%)
  matrix products  17.4 us (9%)
  between operations  13.7 us (7%)
  other arithmetic  7.73 us (4%)
  local copies, waits for them, and re-layouts  4.68 us (2%)
    all_gather x1, waiting for transfers between devices, layer(): all_heads = lax.all_gather(attended, TP_AXES, axis=1, tiled=True)  106 us
    psum x3, blocking collectives, layer(): squares = lax.psum(squares, axis)  20.6 us
    ppermute x2, starting transfers between devices, from_behind(): return lax.ppermute(block, axis, route)  11.4 us
    all_to_all x1, starting transfers between devices, layer(): lax.all_to_all(out_weight.reshape(head_width, n_tp, col_share), TP_AXES,...  9.38 us
    ppermute x2, waiting for transfers between devices, from_behind(): return lax.ppermute(block, axis, route)  7.83 us
    dot_general x1, matrix products, layer(): queries = jnp.dot(normed, query_weight, preferred_element_type=jnp.float32)  5.03 us
    dot_general x1, matrix products, layer(): jnp.dot(normed, keyval_weight, preferred_element_type=jnp.float32)  4.63 us
  transfers between devices with their start and end apart: 5, of which 3 were waited for; matrix products, arithmetic and copies ran while one was open for 9% of the time, Pallas kernels for 0%

profile of v3, /device:TPU:192, one launch (start us, length us, event | category | flops | bytes accessed | tf_op | source)
XLA Modules:
  0.0 202.1 jit_solution(3256761513196848648)
XLA Ops:
  6.5 2.6 %copy.11 = bf16[128,5376]{0,1:T(8,128)(2,1)} copy(bf16[128,5376]{1,0:T(8,128)(2,1)} %param.14) | data formatting | bytes 2752512 | tf_op args[6]
  9.1 9.4 %all-to-all-start = ((bf16[128,24,224]{0,2,1:T(8,128)(2,1)}), bf16[128,24,224]{0,2,1:T(8,128)(2,1)S(1)}, u32[]{:S(2)}, u32[]{:S(2)}) async-start(bf16[128,24,224]{0,2,1:T(8,128)(2,1)} %bitcast.16), calls=%async_computation | async-start | bytes 2752512 | tf_op jit(solution)/shard_map/all_to_all | solution.py:70
  18.5 0.0 all-gather.2.cloned.1.call-start
  18.6 3.7 %fusion = f32[512]{0:T(512)S(1)} fusion(bf16[512,5376]{1,0:T(8,128)(2,1)} %param.8), kind=kLoop, calls=%fused_computation.2 | loop fusion | flops 8257024 | bytes 5507072 | tf_op jit(solution)/shard_map/reduce_sum | solution.py:41
  22.4 0.0 copy-start.1
  22.4 4.6 %multiply_reduce_fusion.1 = (f32[512]{0:T(512)S(1)}, f32[512,128]{0,1:T(8,128)S(1)}) fusion(bf16[5376,128]{1,0:T(8,128)(2,1)S(1)} %copy-done, bf16[512,5376]{1,0:T(8,128)(2,1)} %param.8, f32[5376]{0:T(1024)S(1)} %copy-done.4, f32[512]{0:T(512)S(1)} %add_rsqrt_fusion.3), kind=kOutput, calls=%fused_computation.38 | convolution fusion | flops 715783680 | bytes 7169024 | tf_op jit(solution)/shard_map/dot_general | solution.py:66
  27.0 0.5 multiply_sine_fusion
  27.6 0.1 multiply_multiply_fusion
  27.7 0.1 fusion.23
  27.8 9.4 %collective-permute-start = (bf16[512,128]{0,1:T(8,128)(2,1)S(1)}, bf16[512,128]{0,1:T(8,128)(2,1)S(1)}, u32[]{:S(2)}, u32[]{:S(2)}) collective-permute-start(bf16[512,128]{0,1:T(8,128)(2,1)S(1)} %fusion.23), channel_id=1, source_target_pairs={{0,48},{24,72},{48,96},{72,120},{96,144},{120,168},{144,192},{168,... | collective-permute-start | bytes 393224 | tf_op jit(solution)/shard_map/ppermute | solution.py:19
  37.3 1.9 collective-permute-start.1
  39.2 0.0 copy-start.3
  39.2 5.0 %multiply_reduce_fusion.2 = (f32[512]{0:T(512)S(1)}, f32[512,128]{0,1:T(8,128)S(1)}) fusion(bf16[5376,128]{1,0:T(8,128)(2,1)} %param.10, bf16[512,5376]{1,0:T(8,128)(2,1)} %param.8, f32[5376]{0:T(1024)S(1)} %copy-done.4, f32[512]{0:T(512)S(1)} %add_rsqrt_fusion.3), kind=kOutput, calls=%fused_computation.40 | convolution fusion | flops 715783680 | bytes 7169024 | tf_op jit(solution)/shard_map/dot_general | solution.py:83
  44.3 0.1 multiply_multiply_fusion.1
  44.4 7.8 %collective-permute-done.1 = bf16[512,128]{0,1:T(8,128)(2,1)} collective-permute-done((bf16[512,128]{0,1:T(8,128)(2,1)S(1)}, bf16[512,128]{0,1:T(8,128)(2,1)}, u32[]{:S(2)}, u32[]{:S(2)}) %collective-permute-start.1) | collective-permute-done | bytes 131104 | tf_op jit(solution)/shard_map/ppermute | solution.py:19
  52.2 1.7 pad_maximum_fusion
  53.9 1.9 collective-permute-start.2
  55.9 0.5 copy.12
  56.4 0.2 copy.16
  56.7 1.2 collective-permute-done.2
  57.8 2.4 %fusion.30 = (f32[512]{0:T(512)S(1)}, f32[512,1536]{1,0:T(8,128)S(1)}) fusion(bf16[1536,128]{0,1:T(8,128)(2,1)} %pad_maximum_fusion, bf16[1536,128]{0,1:T(8,128)(2,1)} %collective-permute-done.2, pred[]{:T(512)S(6)} %eq.3, f32[512,128]{0,1:T(8,128)S(1)} %multiply_multiply_fusion.1, f32[512,64]{0,1:T(8,128)S(1)} %get-tuple-element.16, ...), kind=kOutput, calls=%fused_computation.58 | convolution fusion | flops 207552000 | bytes 4730369 | tf_op jit(solution)/shard_map/dot_general | solution.py:91
  60.2 0.6 fusion.5
  60.8 2.4 %fusion.11 = bf16[512,128]{1,0:T(8,128)(2,1)} fusion(f32[512,1536]{1,0:T(8,128)S(1)} %get-tuple-element.22, f32[512]{0:T(512)S(1)} %fusion.5, f32[512]{0:T(512)S(1)} %get-tuple-element.21, bf16[1536,128]{0,1:T(8,128)(2,1)} %collective-permute-done.2, bf16[1536,128]{0,1:T(8,128)(2,1)} %pad_maximum_fusion, pred[]{:T(512)S(6)} %eq.3), kind=kOutput, calls=%fused_computation.17 | convolution fusion | flops 203948032 | bytes 4067329 | tf_op jit(solution)/shard_map/dot_general | solution.py:101
  63.2 0.0 all-gather.2.cloned.1.call-update
  63.2 1.1 constant_dynamic-slice_fusion
  64.4 0.1 copy.13
  64.5 106.2 %all-gather.2.cloned.1.call-done = bf16[512,3072]{1,0:T(8,128)(2,1)} async-done(((bf16[512,128]{1,0:T(8,128)(2,1)}), bf16[512,3072]{1,0:T(8,128)(2,1)}) %all-gather.2.cloned.1.call-update) | async-done | bytes 3145744 | tf_op jit(solution)/shard_map/all_gather | solution.py:105
  170.8 3.0 %multiply_reduce_fusion = (f32[512]{0:T(512)S(1)}, f32[512,224]{0,1:T(8,128)S(1)}) fusion(bf16[512,3072]{1,0:T(8,128)(2,1)} %all-gather.2.cloned.1.call-done, bf16[3072,224]{0,1:T(8,128)(2,1)S(1)} %bitcast.18), kind=kOutput, calls=%fused_computation.19 | convolution fusion | flops 704871936 | bytes 4982784 | tf_op jit(solution)/shard_map/dot_general | solution.py:106
  173.8 2.5 %psum.21 = f32[512]{0:T(512)S(1)} all-reduce(f32[512]{0:T(512)S(1)} %get-tuple-element.23), channel_id=1, replica_groups=mesh['ctx'=32,'zl'=3,'x'=4,'core'=2] {'core'}, use_global_device_ids=true, to_apply=%region_6.7 | all-reduce | flops 512 | bytes 4096 | tf_op jit(solution)/shard_map/psum | solution.py:109
  176.3 7.7 %psum.22 = f32[512]{0:T(512)S(1)} all-reduce(f32[512]{0:T(512)S(1)} %psum.21), channel_id=1, replica_groups=mesh['ctx'=32,'zl'=3,'x'=4,'core'=2] {'x'}, use_global_device_ids=true, to_apply=%region_7.8 | all-reduce | flops 512 | bytes 4096 | tf_op jit(solution)/shard_map/psum | solution.py:109
  184.0 10.4 %psum.23 = f32[512]{0:T(512)S(1)} all-reduce(f32[512]{0:T(512)S(1)} %psum.22), channel_id=1, replica_groups=mesh['ctx'=32,'zl'=3,'x'=4,'core'=2] {'zl'}, use_global_device_ids=true, to_apply=%region_8.9 | all-reduce | flops 512 | bytes 4096 | tf_op jit(solution)/shard_map/psum | solution.py:109
  194.4 0.8 add_convert_fusion
  (20 shorter events, 0.1 us)
Async XLA Ops:
  6.5 15.8 %copy-start = (bf16[5376,128]{1,0:T(8,128)(2,1)S(1)}, bf16[5376,128]{1,0:T(8,128)(2,1)}, u32[]{:S(2)}) copy-start(bf16[5376,128]{1,0:T(8,128)(2,1)} %param.11) | copy-start | bytes 4128772
  9.1 46.7 %all-to-all-start = ((bf16[128,24,224]{0,2,1:T(8,128)(2,1)}), bf16[128,24,224]{0,2,1:T(8,128)(2,1)S(1)}, u32[]{:S(2)}, u32[]{:S(2)}) async-start(bf16[128,24,224]{0,2,1:T(8,128)(2,1)} %bitcast.16), calls=%async_computation | async-start | bytes 2752512 | tf_op jit(solution)/shard_map/all_to_all | solution.py:70
  18.5 3.8 %copy-start.4 = (f32[5376]{0:T(1024)S(1)}, f32[5376]{0:T(1024)}, u32[]{:S(2)}) copy-start(f32[5376]{0:T(1024)} %param.9) | copy-start | bytes 64516
  18.5 152.2 %all-gather.2.cloned.1.call-start = ((), (), s32[]{:S(2)}) async-start(), calls=%async_computation.1 | async-start | bytes 3276800 | tf_op jit(solution)/shard_map/all_gather | solution.py:105
  22.4 5.2 %copy-start.1 = (f32[128]{0:T(128)S(1)}, f32[128]{0:T(128)}, u32[]{:S(2)}) copy-start(f32[128]{0:T(128)} %param.13) | copy-start | bytes 1540
  27.8 16.5 %collective-permute-start = (bf16[512,128]{0,1:T(8,128)(2,1)S(1)}, bf16[512,128]{0,1:T(8,128)(2,1)S(1)}, u32[]{:S(2)}, u32[]{:S(2)}) collective-permute-start(bf16[512,128]{0,1:T(8,128)(2,1)S(1)} %fusion.23), channel_id=1, source_target_pairs={{0,48},{24,72},{48,96},{72,120},{96,144},{120,168},{144,192},{168,... | collective-permute-start | bytes 393224 | tf_op jit(solution)/shard_map/ppermute | solution.py:19
  37.3 14.9 %collective-permute-start.1 = (bf16[512,128]{0,1:T(8,128)(2,1)S(1)}, bf16[512,128]{0,1:T(8,128)(2,1)}, u32[]{:S(2)}, u32[]{:S(2)}) collective-permute-start(bf16[512,128]{0,1:T(8,128)(2,1)S(1)} %fusion.23), channel_id=1, source_target_pairs={{0,24},{24,48},{48,72},{72,96},{96,120},{120,144},{144,168},{168,1... | collective-permute-start | bytes 393224 | tf_op jit(solution)/shard_map/ppermute | solution.py:19
  39.2 5.1 %copy-start.3 = (f32[128]{0:T(128)S(1)}, f32[128]{0:T(128)}, u32[]{:S(2)}) copy-start(f32[128]{0:T(128)} %param.12) | copy-start | bytes 1540
  53.9 3.9 %collective-permute-start.2 = (bf16[1536,128]{0,1:T(8,128)(2,1)}, bf16[1536,128]{0,1:T(8,128)(2,1)}, u32[]{:S(2)}, u32[]{:S(2)}) collective-permute-start(bf16[1536,128]{0,1:T(8,128)(2,1)} %pad_maximum_fusion), channel_id=1, source_target_pairs={{0,1},{1,0},{2,3},{3,2},{4,5},{5,4},{6,7},{7,6},{8,9},{9,8},{10,11... | collective-permute-start | bytes 1179656 | tf_op jit(solution)/shard_map/ppermute | solution.py:76
  64.3 130.1 %copy-start.2 = (f32[224]{0:T(256)S(1)}, f32[224]{0:T(256)}, u32[]{:S(2)}) copy-start(f32[224]{0:T(256)} %param.15) | copy-start | bytes 2692
Sparse Core Ops, SparseCore 0:
  63.3 107.3 all-gather.1

commit v4 on v3

--- a/solution.py
+++ b/solution.py
@@ -102,11 +102,17 @@
         jnp.bfloat16
     )
 
-    all_heads = lax.all_gather(attended, TP_AXES, axis=1, tiled=True)
-    summed = jnp.dot(all_heads, weight_block, preferred_element_type=jnp.float32)
+    copies = jnp.broadcast_to(attended[None], (n_tp,) + attended.shape)
+    all_heads = lax.all_to_all(copies, TP_AXES, 0, 0, tiled=True)
+    summed = lax.dot_general(
+        all_heads,
+        weight_block.reshape(n_tp, head_width, col_share),
+        (((0, 2), (0, 1)), ((), ())),
+        preferred_element_type=jnp.float32,
+    )
     squares = jnp.sum(summed * summed, axis=1)
-    for axis in ("core", "x", "zl"):
-        squares = lax.psum(squares, axis)
+    square_copies = jnp.broadcast_to(squares[None], (n_tp,) + squares.shape)
+    squares = jnp.sum(lax.all_to_all(square_copies, TP_AXES, 0, 0, tiled=True), axis=0)
     scaled = summed * lax.rsqrt(squares[:, None] / model_width + epsilon) * post_gain
     residual = lax.dynamic_slice_in_dim(tokens, tp_index * col_share, col_share, 1)
     return (residual.astype(jnp.float32) + scaled).astype(jnp.bfloat16)

time: 203 us -> 141 us (0.69)
  the two profiles are of different devices: /device:TPU:192 before, /device:TPU:56 now
where the time goes in v4:
time: 141 us; the launch traced here: 140 us
  blocking collectives  60.4 us (43%)
  starting transfers between devices  32.4 us (23%)
  waiting for transfers between devices  18.2 us (13%)
  matrix products  14.9 us (11%)
  other arithmetic  7.79 us (6%)
  local copies, waits for them, and re-layouts  6 us (4%)
    all_to_all x1, blocking collectives, layer(): all_heads = lax.all_to_all(copies, TP_AXES, 0, 0, tiled=True)  60.4 us
    ppermute x2, starting transfers between devices, from_behind(): return lax.ppermute(block, axis, route)  18.5 us
    ppermute x2, waiting for transfers between devices, from_behind(): return lax.ppermute(block, axis, route)  11.3 us
    all_to_all x1, starting transfers between devices, layer(): lax.all_to_all(out_weight.reshape(head_width, n_tp, col_share), TP_AXES,...  8.17 us
    all_to_all x1, waiting for transfers between devices, layer(): lax.all_to_all(square_copies, TP_AXES, 0, 0, tiled=True)  5.75 us
    dot_general x1, matrix products, layer(): queries = jnp.dot(normed, query_weight, preferred_element_type=jnp.float32)  5.03 us
    dot_general x1, matrix products, layer(): jnp.dot(normed, keyval_weight, preferred_element_type=jnp.float32)  4.63 us
    all_to_all x1, starting transfers between devices, layer(): lax.all_to_all(square_copies, TP_AXES, 0, 0, tiled=True)  3.82 us
  transfers between devices with their start and end apart: 5, of which 4 were waited for; matrix products, arithmetic and copies ran while one was open for 13% of the time, Pallas kernels for 0%

profile of v4, /device:TPU:56, one launch (start us, length us, event | category | flops | bytes accessed | tf_op | source)
XLA Modules:
  0.0 140.0 jit_solution(2692065125646703678)
XLA Ops:
  0.0 2.6 %copy.19 = bf16[128,5376]{0,1:T(8,128)(2,1)} copy(bf16[128,5376]{1,0:T(8,128)(2,1)} %param.14) | data formatting | bytes 2752512 | tf_op args[6]
  2.6 8.2 %all-to-all-start = ((bf16[128,24,224]{0,2,1:T(8,128)(2,1)}), bf16[128,24,224]{0,2,1:T(8,128)(2,1)S(1)}, u32[]{:S(2)}, u32[]{:S(2)}) async-start(bf16[128,24,224]{0,2,1:T(8,128)(2,1)} %bitcast.28), calls=%async_computation | async-start | bytes 2752512 | tf_op jit(solution)/shard_map/all_to_all | solution.py:70
  10.8 0.0 copy-start.4
  10.8 3.7 %fusion = f32[512]{0:T(512)S(1)} fusion(bf16[512,5376]{1,0:T(8,128)(2,1)} %param.8), kind=kLoop, calls=%fused_computation.2 | loop fusion | flops 8257024 | bytes 5507072 | tf_op jit(solution)/shard_map/reduce_sum | solution.py:41
  14.6 4.6 %multiply_reduce_fusion.1 = (f32[512]{0:T(512)S(1)}, f32[512,128]{0,1:T(8,128)S(1)}) fusion(bf16[5376,128]{1,0:T(8,128)(2,1)S(1)} %copy-done, bf16[512,5376]{1,0:T(8,128)(2,1)} %param.8, f32[5376]{0:T(1024)S(1)} %copy-done.4, f32[512]{0:T(512)S(1)} %add_rsqrt_fusion.3), kind=kOutput, calls=%fused_computation.42 | convolution fusion | flops 715783680 | bytes 7169024 | tf_op jit(solution)/shard_map/dot_general | solution.py:66
  19.2 0.5 multiply_sine_fusion
  19.8 0.1 multiply_multiply_fusion
  19.9 0.1 fusion.29
  20.0 13.9 %collective-permute-start = (bf16[512,128]{0,1:T(8,128)(2,1)S(1)}, bf16[512,128]{0,1:T(8,128)(2,1)S(1)}, u32[]{:S(2)}, u32[]{:S(2)}) collective-permute-start(bf16[512,128]{0,1:T(8,128)(2,1)S(1)} %fusion.29), channel_id=1, source_target_pairs={{0,48},{24,72},{48,96},{72,120},{96,144},{120,168},{144,192},{168,... | collective-permute-start | bytes 393224 | tf_op jit(solution)/shard_map/ppermute | solution.py:19
  34.0 4.6 %collective-permute-start.1 = (bf16[512,128]{0,1:T(8,128)(2,1)S(1)}, bf16[512,128]{0,1:T(8,128)(2,1)}, u32[]{:S(2)}, u32[]{:S(2)}) collective-permute-start(bf16[512,128]{0,1:T(8,128)(2,1)S(1)} %fusion.29), channel_id=1, source_target_pairs={{0,24},{24,48},{48,72},{72,96},{96,120},{120,144},{144,168},{168,1... | collective-permute-start | bytes 393224 | tf_op jit(solution)/shard_map/ppermute | solution.py:19
  38.6 5.0 %multiply_reduce_fusion.2 = (f32[512]{0:T(512)S(1)}, f32[512,128]{0,1:T(8,128)S(1)}) fusion(bf16[5376,128]{1,0:T(8,128)(2,1)} %param.10, bf16[512,5376]{1,0:T(8,128)(2,1)} %param.8, f32[5376]{0:T(1024)S(1)} %copy-done.4, f32[512]{0:T(512)S(1)} %add_rsqrt_fusion.3), kind=kOutput, calls=%fused_computation.44 | convolution fusion | flops 715783680 | bytes 7169024 | tf_op jit(solution)/shard_map/dot_general | solution.py:83
  43.7 0.1 multiply_multiply_fusion.1
  43.8 9.7 %collective-permute-done = bf16[512,128]{0,1:T(8,128)(2,1)S(1)} collective-permute-done((bf16[512,128]{0,1:T(8,128)(2,1)S(1)}, bf16[512,128]{0,1:T(8,128)(2,1)S(1)}, u32[]{:S(2)}, u32[]{:S(2)}) %collective-permute-start) | collective-permute-done | bytes 131104 | tf_op jit(solution)/shard_map/ppermute | solution.py:19
  53.4 1.6 %collective-permute-done.1 = bf16[512,128]{0,1:T(8,128)(2,1)} collective-permute-done((bf16[512,128]{0,1:T(8,128)(2,1)S(1)}, bf16[512,128]{0,1:T(8,128)(2,1)}, u32[]{:S(2)}, u32[]{:S(2)}) %collective-permute-start.1) | collective-permute-done | bytes 131104 | tf_op jit(solution)/shard_map/ppermute | solution.py:19
  55.0 1.7 %pad_maximum_fusion = bf16[1536,128]{0,1:T(8,128)(2,1)} fusion(bf16[512,128]{0,1:T(8,128)(2,1)S(1)} %fusion.29, bf16[512,128]{0,1:T(8,128)(2,1)} %collective-permute-done.1, bf16[512,128]{0,1:T(8,128)(2,1)S(1)} %collective-permute-done), kind=kLoop, calls=%fused_computation.24 | loop fusion | flops 1179648 | bytes 786432 | tf_op jit(solution)/shard_map/concatenate | solution.py:75
  56.7 1.9 %collective-permute-start.2 = (bf16[1536,128]{0,1:T(8,128)(2,1)}, bf16[1536,128]{0,1:T(8,128)(2,1)}, u32[]{:S(2)}, u32[]{:S(2)}) collective-permute-start(bf16[1536,128]{0,1:T(8,128)(2,1)} %pad_maximum_fusion), channel_id=1, source_target_pairs={{0,1},{1,0},{2,3},{3,2},{4,5},{5,4},{6,7},{7,6},{8,9},{9,8},{10,11... | collective-permute-start | bytes 1179656 | tf_op jit(solution)/shard_map/ppermute | solution.py:76
  58.7 0.5 copy.20
  59.2 0.2 copy.36
  59.5 1.2 collective-permute-done.2
  60.7 2.4 %fusion.36 = (f32[512]{0:T(512)S(1)}, f32[512,1536]{1,0:T(8,128)S(1)}) fusion(bf16[1536,128]{0,1:T(8,128)(2,1)} %pad_maximum_fusion, bf16[1536,128]{0,1:T(8,128)(2,1)} %collective-permute-done.2, pred[]{:T(512)S(6)} %eq.3, f32[512,128]{0,1:T(8,128)S(1)} %multiply_multiply_fusion.1, f32[512,64]{0,1:T(8,128)S(1)} %get-tuple-element.16, ...), kind=kOutput, calls=%fused_computation.62 | convolution fusion | flops 207552000 | bytes 4730369 | tf_op jit(solution)/shard_map/dot_general | solution.py:91
  63.0 0.6 fusion.5
  63.6 1.7 %fusion.17 = bf16[512,128]{1,0:T(8,128)(2,1)S(1)} fusion(f32[512,1536]{1,0:T(8,128)S(1)} %get-tuple-element.22, f32[512]{0:T(512)S(1)} %fusion.5, f32[512]{0:T(512)S(1)} %get-tuple-element.21, bf16[1536,128]{0,1:T(8,128)(2,1)} %collective-permute-done.2, bf16[1536,128]{0,1:T(8,128)(2,1)} %pad_maximum_fusion, pred[]{:T(512)S(6)} %eq.3), kind=kOutput, calls=%fused_computation.21 | convolution fusion | flops 203948032 | bytes 4067329 | tf_op jit(solution)/shard_map/dot_general | solution.py:101
  65.3 0.7 broadcast_in_dim.8
  66.0 60.4 %all_to_all.26 = bf16[24,512,128]{2,1,0:T(8,128)(2,1)S(1)} all-to-all(bf16[24,512,128]{2,1,0:T(8,128)(2,1)S(1)} %broadcast_in_dim.8), channel_id=1, replica_groups=mesh['ctx'=32,'zl'=3,'x'=4,'core'=2] {'zl','x','core'}, dimensions={0} | all-to-all | bytes 6291456 | tf_op jit(solution)/shard_map/all_to_all | solution.py:106
  126.4 1.1 multiply_reduce_fusion
  127.5 0.7 broadcast_in_dim.9
  128.2 3.8 %all-to-all-start.2 = ((f32[24,1,512]{2,1,0:T(1,128)}), f32[24,1,512]{2,1,0:T(1,128)S(1)}, u32[]{:S(2)}, u32[]{:S(2)}) async-start(f32[24,1,512]{2,1,0:T(1,128)} %broadcast_in_dim.9), calls=%async_computation.2 | async-start | bytes 98304 | tf_op jit(solution)/shard_map/all_to_all | solution.py:115
  132.0 1.1 constant_dynamic-slice_fusion
  133.2 0.1 copy.24
  133.3 5.8 %all-to-all-done.2 = f32[24,1,512]{2,1,0:T(1,128)S(1)} async-done(((f32[24,1,512]{2,1,0:T(1,128)}), f32[24,1,512]{2,1,0:T(1,128)S(1)}, u32[]{:S(2)}, u32[]{:S(2)}) %all-to-all-start.2) | async-done | bytes 49184 | tf_op jit(solution)/shard_map/all_to_all | solution.py:115
  139.1 0.1 reduce_sum.59
  139.1 0.8 add_convert_fusion
  (20 shorter events, 0.1 us)
Async XLA Ops:
  0.0 14.6 %copy-start = (bf16[5376,128]{1,0:T(8,128)(2,1)S(1)}, bf16[5376,128]{1,0:T(8,128)(2,1)}, u32[]{:S(2)}) copy-start(bf16[5376,128]{1,0:T(8,128)(2,1)} %param.11) | copy-start | bytes 4128772
  2.6 56.1 %all-to-all-start = ((bf16[128,24,224]{0,2,1:T(8,128)(2,1)}), bf16[128,24,224]{0,2,1:T(8,128)(2,1)S(1)}, u32[]{:S(2)}, u32[]{:S(2)}) async-start(bf16[128,24,224]{0,2,1:T(8,128)(2,1)} %bitcast.28), calls=%async_computation | async-start | bytes 2752512 | tf_op jit(solution)/shard_map/all_to_all | solution.py:70
  10.8 3.8 %copy-start.4 = (f32[5376]{0:T(1024)S(1)}, f32[5376]{0:T(1024)}, u32[]{:S(2)}) copy-start(f32[5376]{0:T(1024)} %param.9) | copy-start | bytes 64516
  14.6 5.2 %copy-start.1 = (f32[128]{0:T(128)S(1)}, f32[128]{0:T(128)}, u32[]{:S(2)}) copy-start(f32[128]{0:T(128)} %param.13) | copy-start | bytes 1540
  20.0 33.4 %collective-permute-start = (bf16[512,128]{0,1:T(8,128)(2,1)S(1)}, bf16[512,128]{0,1:T(8,128)(2,1)S(1)}, u32[]{:S(2)}, u32[]{:S(2)}) collective-permute-start(bf16[512,128]{0,1:T(8,128)(2,1)S(1)} %fusion.29), channel_id=1, source_target_pairs={{0,48},{24,72},{48,96},{72,120},{96,144},{120,168},{144,192},{168,... | collective-permute-start | bytes 393224 | tf_op jit(solution)/shard_map/ppermute | solution.py:19
  34.0 21.0 %collective-permute-start.1 = (bf16[512,128]{0,1:T(8,128)(2,1)S(1)}, bf16[512,128]{0,1:T(8,128)(2,1)}, u32[]{:S(2)}, u32[]{:S(2)}) collective-permute-start(bf16[512,128]{0,1:T(8,128)(2,1)S(1)} %fusion.29), channel_id=1, source_target_pairs={{0,24},{24,48},{48,72},{72,96},{96,120},{120,144},{144,168},{168,1... | collective-permute-start | bytes 393224 | tf_op jit(solution)/shard_map/ppermute | solution.py:19
  38.6 5.1 %copy-start.3 = (f32[128]{0:T(128)S(1)}, f32[128]{0:T(128)}, u32[]{:S(2)}) copy-start(f32[128]{0:T(128)} %param.12) | copy-start | bytes 1540
  56.7 3.9 %collective-permute-start.2 = (bf16[1536,128]{0,1:T(8,128)(2,1)}, bf16[1536,128]{0,1:T(8,128)(2,1)}, u32[]{:S(2)}, u32[]{:S(2)}) collective-permute-start(bf16[1536,128]{0,1:T(8,128)(2,1)} %pad_maximum_fusion), channel_id=1, source_target_pairs={{0,1},{1,0},{2,3},{3,2},{4,5},{5,4},{6,7},{7,6},{8,9},{9,8},{10,11... | collective-permute-start | bytes 1179656 | tf_op jit(solution)/shard_map/ppermute | solution.py:76
  126.4 12.7 %copy-start.2 = (f32[224]{0:T(256)S(1)}, f32[224]{0:T(256)}, u32[]{:S(2)}) copy-start(f32[224]{0:T(256)} %param.15) | copy-start | bytes 2692
  128.2 10.9 %all-to-all-start.2 = ((f32[24,1,512]{2,1,0:T(1,128)}), f32[24,1,512]{2,1,0:T(1,128)S(1)}, u32[]{:S(2)}, u32[]{:S(2)}) async-start(f32[24,1,512]{2,1,0:T(1,128)} %broadcast_in_dim.9), calls=%async_computation.2 | async-start | bytes 98304 | tf_op jit(solution)/shard_map/all_to_all | solution.py:115
